TPU v7x, 128 devices: a whole 4x4x4 slice. The times are simulated.
128 devices in a mesh: tm: 4 (over x), space: 16 (over z, y), ens: 2 (over core).
Axes of the slice: x: 4, y: 4, z: 4, core: 2. Of those that a mesh axis runs over, the one named last changes fastest.
Arguments:
- start_states: float32 [4, 16, 1024, 1024], P('tm', 'ens', 'space'), may hold values from -6 to 6
- velocity_x: float32 [1024, 1024], P('space'), may hold values from -0.15 to 0.15
- velocity_y: float32 [1024, 1024], P('space'), may hold values from -0.15 to 0.15
- diffusivity: float32 [1024, 1024], P('space'), may hold values from 0.06 to 0.2
- source_shape: float32 [1024, 1024], P('space'), may hold values from -6 to 6
- params: float32 [16, 128], P('ens'), may hold values from -6 to 6
- obs_cell: int32 [4, 1024], P('tm', 'space'), may hold values from 0 to 1048575, as said below
- obs_data: float32 [4, 1024], P('tm', 'space'), may hold values from -6 to 6
- obs_noise: float32 [4, 1024, 16], P('tm', 'space'), may hold values from -6 to 6
- obs_var: float32 [4, 1024], P('tm', 'space'), may hold values from 0.05 to 0.5
Outputs:
- new_states: float32 [4, 16, 1024, 1024], P('tm', 'ens', 'space')
- new_params: float32 [16, 128], P('ens')
Inputs may be any that keep to these rules, and one draw needn't show every extreme that they name: `obs_cell`: entry (n, o) lies in the rows of slab o // 64, that is row (o // 64) * 64 up to 63 rows further.
All inputs are finite; a program needn't handle non-finite values.
Results may differ from a plain program's by a relative error of at most 0.0003.
Values sent between devices are 32-bit elements; how exact they have to be, the bound alone decides.
No kernel may reach another device: no remote copies, remote signals or barrier semaphores. Data moves between devices by JAX's collectives and lax.ppermute only.
A program may use at most 128 MiB of HBM per device.

v0:
```python
import math
import jax
import jax.numpy as jnp
from jax import lax
from jax.sharding import PartitionSpec as P

FINE = 4
FINE_DT = 0.25


def with_halo(cells, sides, width):
    for axis, dim in sides:
        count = lax.axis_size(axis)
        ends = count - 1
        head = lax.slice_in_dim(cells, 0, width, axis=dim)
        tail = lax.slice_in_dim(cells, cells.shape[dim] - width, cells.shape[dim], axis=dim)
        cells = jnp.concatenate(
            [
                lax.ppermute(tail, axis, [(i, (i + 1) % count) for i in range(ends)]),
                cells,
                lax.ppermute(head, axis, [((i + 1) % count, i) for i in range(ends)]),
            ],
            axis=dim,
        )
    return cells


def shifted(value, axis, steps):
    count = lax.axis_size(axis)
    first, last = (max(0, -steps), min(count, count - steps))
    return lax.ppermute(value, axis, [(source, source + steps) for source in range(first, last)])


def advance(values_in, coeffs, inside, step_size, forcing):
    middle = values_in[:, 1:-1, :]
    above_row = values_in[:, :-2, :]
    below_row = values_in[:, 2:, :]
    west_cell = jnp.pad(middle[:, :, :-1], ((0, 0), (0, 0), (1, 0)))
    east_cell = jnp.pad(middle[:, :, 1:], ((0, 0), (0, 0), (0, 1)))
    spread_term = coeffs[0] * (above_row + below_row + west_cell + east_cell - 4.0 * middle)
    tendency = (
        spread_term
        - coeffs[1] * (east_cell - west_cell) * 0.5
        - coeffs[2] * (below_row - above_row) * 0.5
    )
    if forcing is not None:
        tendency = tendency + forcing
    return (middle + step_size * tendency) * inside


def row_inside(first_row, count, total_rows):
    global_rows = first_row + jnp.arange(count, dtype=jnp.int32)
    return ((global_rows >= 0) & (global_rows < total_rows)).astype(jnp.float32)[:, None]


def per_device(
    start_states,
    velocity_x,
    velocity_y,
    diffusivity,
    source_shape,
    params,
    obs_cell,
    obs_data,
    obs_noise,
    obs_var,
):
    coarse_dt = FINE_DT * FINE
    state = start_states[0]
    members_here, row_count, col_count = state.shape
    slabs = row_count * lax.axis_size("space")
    first_row = lax.axis_index("space") * row_count
    slice_index = lax.axis_index("tm")
    band_width = col_count // params.shape[1]
    spread_params = jnp.repeat(params, band_width, axis=1)
    coeffs = jnp.stack([diffusivity, velocity_x, velocity_y])
    own_rows = row_inside(first_row, row_count, slabs)
    forcing = source_shape[None] * spread_params[:, None, :]
    current = state
    coarse_part = state
    for section in range(FINE):
        padded = with_halo(current, (("space", 1),), 1)
        if section == 0:
            coarse_part = advance(padded, coeffs, own_rows, coarse_dt, None)
        current = advance(padded, coeffs, own_rows, FINE_DT, forcing)
    correction = jnp.where(slice_index > 0, current - coarse_part, current)
    running = correction
    for link in range(lax.axis_size("tm") - 1):
        earlier = shifted(running, "tm", 1)
        padded = with_halo(earlier, (("space", 1),), 1)
        running = correction + advance(padded, coeffs, own_rows, coarse_dt, None)
    new_states = running[None]
    flat = running.reshape(members_here, row_count * col_count)
    local_cell = obs_cell[0] - first_row * col_count
    predicted = jnp.take(flat, local_cell, axis=1)
    every_pred, every_param = (
        lax.all_gather(predicted, "ens", axis=0, tiled=True),
        lax.all_gather(params, "ens", axis=0, tiled=True),
    )
    total = every_pred.shape[0]
    norm_factor = 1.0 / math.sqrt(total - 1)
    inv_spread = lax.rsqrt(obs_var[0])[None, :]
    pred_mean = jnp.mean(every_pred, axis=0, keepdims=True)
    anomaly = (every_pred - pred_mean) * (inv_spread * norm_factor)
    misfit = (obs_data[0][None, :] + obs_noise[0].T - every_pred) * inv_spread
    gram = jnp.dot(anomaly, anomaly.T, precision=lax.Precision.HIGHEST)
    cross = jnp.dot(anomaly, misfit.T, precision=lax.Precision.HIGHEST)
    gram, cross = lax.psum((gram, cross), ("tm", "space"))
    system = jnp.eye(total, dtype=jnp.float32) + gram
    factor = jnp.linalg.cholesky(system)
    weights = jax.scipy.linalg.cho_solve((factor, True), cross)
    param_anom = every_param - jnp.mean(every_param, axis=0)
    own_weights = lax.dynamic_slice_in_dim(
        weights, lax.axis_index("ens") * members_here, members_here, 1
    )
    new_params = (
        params + jnp.dot(own_weights.T, param_anom, precision=lax.Precision.HIGHEST) * norm_factor
    )
    return (new_states, new_params)


def solution(mesh):
    in_specs = (
        P("tm", "ens", "space", None),
        P("space", None),
        P("space", None),
        P("space", None),
        P("space", None),
        P("ens", None),
        P("tm", "space"),
        P("tm", "space"),
        P("tm", "space", None),
        P("tm", "space"),
    )
    out_specs = (P("tm", "ens", "space", None), P("ens", None))
    return jax.shard_map(
        per_device, mesh=mesh, in_specs=in_specs, out_specs=out_specs, check_vma=False
    )
```

profile of v0, /device:TPU:0, one launch (start us, length us, event | category | flops | bytes accessed | tf_op | source)
XLA Modules:
  0.0 608.6 jit_solution(10801937823309952952)
XLA Ops:
  1.7 3.6 collective-permute-start
  6.7 5.1 fusion.52
  14.2 3.4 fusion.2
  17.7 4.5 collective-permute-start.2
  24.4 3.7 collective-permute-done.3
  30.2 3.5 collective-permute-start.4
  35.8 4.6 collective-permute-done.5
  42.6 6.0 collective-permute-start.6
  51.0 3.7 collective-permute-done.7
  54.7 4.7 subtract_select_fusion
  59.4 3.5 collective-permute-start.8
  63.0 40.2 %collective-permute-done.8 = f32[8,64,1024]{2,1,0:T(8,128)S(1)} collective-permute-done((f32[8,64,1024]{2,1,0:T(8,128)S(1)}, f32[8,64,1024]{2,1,0:T(8,128)S(1)}, u32[]{:S(2)}, u32[]{:S(2)}) %collective-permute-start.8) | collective-permute-done | bytes 2097184 | tf_op jit(solution)/shard_map/ppermute | solution.py:31
  104.5 5.2 collective-permute-start.9
  113.2 4.7 collective-permute-start.11
  117.9 38.7 %collective-permute-done.11 = f32[8,64,1024]{2,1,0:T(8,128)S(1)} collective-permute-done((f32[8,64,1024]{2,1,0:T(8,128)S(1)}, f32[8,64,1024]{2,1,0:T(8,128)S(1)}, u32[]{:S(2)}, u32[]{:S(2)}) %collective-permute-start.11) | collective-permute-done | bytes 2097184 | tf_op jit(solution)/shard_map/ppermute | solution.py:31
  156.7 3.9 collective-permute-start.12
  162.8 3.7 collective-permute-done.13
  169.5 4.5 collective-permute-start.14
  175.9 34.7 %collective-permute-done.14 = f32[8,64,1024]{2,1,0:T(8,128)S(1)} collective-permute-done((f32[8,64,1024]{2,1,0:T(8,128)}, f32[8,64,1024]{2,1,0:T(8,128)S(1)}, u32[]{:S(2)}, u32[]{:S(2)}) %collective-permute-start.14) | collective-permute-done | bytes 2097184 | tf_op jit(solution)/shard_map/ppermute | solution.py:31
  210.6 5.4 collective-permute-start.15
  218.2 5.6 collective-permute-done.16
  226.7 17.9 %copy.18 = f32[8,64,1024]{0,2,1:T(8,128)} copy(f32[8,64,1024]{2,1,0:T(8,128)} %multiply_add_fusion.4) | data formatting | bytes 4194304 | tf_op jit(solution)/shard_map/add | solution.py:91
  244.6 11.1 %gather_fusion = f32[64,8]{1,0:T(8,128)S(1)} fusion(f32[8,65536]{0,1:T(8,128)} %bitcast.43, s32[1024]{0:T(1024)S(1)} %pad_clamp_fusion), kind=kCustom, calls=%fused_computation | custom fusion | bytes 4352 | tf_op jit(solution)/shard_map/jit(_take)/gather | solution.py:95
  258.0 345.3 %all-reduce.14 = (f32[16,16]{1,0:T(8,128)S(1)}, f32[16,16]{1,0:T(8,128)S(1)}) all-reduce(f32[16,16]{1,0:T(8,128)S(1)} %fusion.21, f32[16,16]{1,0:T(8,128)S(1)} %fusion.29), channel_id=1, replica_groups=mesh['tm'=4,'space'=16,'ens'=2] {'tm','space'}, use_global_device_ids=true, to_apply=%region_4.5 | all-reduce | flops 512 | bytes 4096 | tf_op jit(solution)/shard_map/psum | solution.py:108
  (90 shorter events, 40.2 us)
Async XLA Ops:
  1.7 12.4 %collective-permute-start = (f32[8,1,1024]{2,1,0:T(1,128)S(1)}, f32[8,1,1024]{2,1,0:T(1,128)S(1)}, u32[]{:S(2)}, u32[]{:S(2)}) collective-permute-start(f32[8,1,1024]{2,1,0:T(1,128)S(1)} %get-tuple-element.31), channel_id=1, source_target_pairs={{0,2},{2,4},{4,6},{6,8},{8,10},{10,12},{12,14},{14,16},{16,18},{18... | collective-permute-start | bytes 98312 | tf_op jit(solution)/shard_map/ppermute | solution.py:19
  5.3 8.9 %collective-permute-start.1 = (f32[8,1,1024]{2,1,0:T(1,128)S(1)}, f32[8,1,1024]{2,1,0:T(1,128)S(1)}, u32[]{:S(2)}, u32[]{:S(2)}) collective-permute-start(f32[8,1,1024]{2,1,0:T(1,128)S(1)} %get-tuple-element.30), channel_id=1, source_target_pairs={{2,0},{4,2},{6,4},{8,6},{10,8},{12,10},{14,12},{16,14},{18,16},{20... | collective-permute-start | bytes 98312 | tf_op jit(solution)/shard_map/ppermute | solution.py:21
  6.6 7.6 %copy-start = (f32[1,8,64,1024]{3,2,1,0:T(8,128)S(1)}, f32[1,8,64,1024]{3,2,1,0:T(8,128)}, u32[]{:S(2)}) copy-start(f32[1,8,64,1024]{3,2,1,0:T(8,128)} %param.10) | copy-start | bytes 6291460
  17.7 6.7 %collective-permute-start.2 = (f32[8,1,1024]{2,1,0:T(1,128)S(1)}, f32[8,1,1024]{2,1,0:T(1,128)S(1)}, u32[]{:S(2)}, u32[]{:S(2)}) collective-permute-start(f32[8,1,1024]{2,1,0:T(1,128)S(1)} %get-tuple-element.25), channel_id=1, source_target_pairs={{0,2},{2,4},{4,6},{6,8},{8,10},{10,12},{12,14},{14,16},{16,18},{18... | collective-permute-start | bytes 98312 | tf_op jit(solution)/shard_map/ppermute | solution.py:19
  22.3 5.8 collective-permute-start.3
  30.2 5.6 collective-permute-start.4
  33.7 6.8 %collective-permute-start.5 = (f32[8,1,1024]{2,1,0:T(1,128)S(1)}, f32[8,1,1024]{2,1,0:T(1,128)S(1)}, u32[]{:S(2)}, u32[]{:S(2)}) collective-permute-start(f32[8,1,1024]{2,1,0:T(1,128)S(1)} %get-tuple-element.20), channel_id=1, source_target_pairs={{2,0},{4,2},{6,4},{8,6},{10,8},{12,10},{14,12},{16,14},{18,16},{20... | collective-permute-start | bytes 98312 | tf_op jit(solution)/shard_map/ppermute | solution.py:21
  42.6 8.5 %collective-permute-start.6 = (f32[8,1,1024]{2,1,0:T(1,128)S(1)}, f32[8,1,1024]{2,1,0:T(1,128)S(1)}, u32[]{:S(2)}, u32[]{:S(2)}) collective-permute-start(f32[8,1,1024]{2,1,0:T(1,128)S(1)} %get-tuple-element.17), channel_id=1, source_target_pairs={{0,2},{2,4},{4,6},{6,8},{8,10},{10,12},{12,14},{14,16},{16,18},{18... | collective-permute-start | bytes 98312 | tf_op jit(solution)/shard_map/ppermute | solution.py:19
  48.6 6.1 collective-permute-start.7
  59.4 107.1 %copy-start.1 = (f32[8,64,1024]{2,1,0:T(8,128)}, f32[8,64,1024]{2,1,0:T(8,128)S(1)}, u32[]{:S(2)}) copy-start(f32[8,64,1024]{2,1,0:T(8,128)S(1)} %subtract_select_fusion) | copy-start | bytes 6291460
  59.4 43.7 %collective-permute-start.8 = (f32[8,64,1024]{2,1,0:T(8,128)S(1)}, f32[8,64,1024]{2,1,0:T(8,128)S(1)}, u32[]{:S(2)}, u32[]{:S(2)}) collective-permute-start(f32[8,64,1024]{2,1,0:T(8,128)S(1)} %subtract_select_fusion), channel_id=1, source_target_pairs={{0,32},{32,64},{64,96},{1,33},{33,65},{65,97},{2,34},{34,66},{66,9... | collective-permute-start | bytes 6291464 | tf_op jit(solution)/shard_map/ppermute | solution.py:31
  103.2 7.3 %collective-permute-start.10 = (f32[8,1,1024]{2,1,0:T(1,128)S(1)}, f32[8,1,1024]{2,1,0:T(1,128)S(1)}, u32[]{:S(2)}, u32[]{:S(2)}) collective-permute-start(f32[8,1,1024]{2,1,0:T(1,128)S(1)} %get-tuple-element.12), channel_id=1, source_target_pairs={{2,0},{4,2},{6,4},{8,6},{10,8},{12,10},{14,12},{16,14},{18,16},{20... | collective-permute-start | bytes 98312 | tf_op jit(solution)/shard_map/ppermute | solution.py:21
  104.5 6.8 %collective-permute-start.9 = (f32[8,1,1024]{2,1,0:T(1,128)S(1)}, f32[8,1,1024]{2,1,0:T(1,128)S(1)}, u32[]{:S(2)}, u32[]{:S(2)}) collective-permute-start(f32[8,1,1024]{2,1,0:T(1,128)S(1)} %get-tuple-element.13), channel_id=1, source_target_pairs={{0,2},{2,4},{4,6},{6,8},{8,10},{10,12},{12,14},{14,16},{16,18},{18... | collective-permute-start | bytes 98312 | tf_op jit(solution)/shard_map/ppermute | solution.py:19
  113.2 43.4 %collective-permute-start.11 = (f32[8,64,1024]{2,1,0:T(8,128)S(1)}, f32[8,64,1024]{2,1,0:T(8,128)S(1)}, u32[]{:S(2)}, u32[]{:S(2)}) collective-permute-start(f32[8,64,1024]{2,1,0:T(8,128)S(1)} %multiply_add_fusion.6), channel_id=1, source_target_pairs={{0,32},{32,64},{64,96},{1,33},{33,65},{65,97},{2,34},{34,66},{66,9... | collective-permute-start | bytes 6291464 | tf_op jit(solution)/shard_map/ppermute | solution.py:31
  156.7 6.1 collective-permute-start.12
  160.7 5.8 collective-permute-start.13
  166.5 9.3 %copy-start.12 = (s32[1,64]{1,0:T(1,128)S(1)}, s32[1,64]{1,0:T(1,128)}, u32[]{:S(2)}) copy-start(s32[1,64]{1,0:T(1,128)} %param.16) | copy-start | bytes 772
  166.5 9.4 %copy-start.13 = (f32[1,64]{1,0:T(1,128)S(1)}, f32[1,64]{1,0:T(1,128)}, u32[]{:S(2)}) copy-start(f32[1,64]{1,0:T(1,128)} %param.19) | copy-start | bytes 772
  169.5 41.1 %collective-permute-start.14 = (f32[8,64,1024]{2,1,0:T(8,128)}, f32[8,64,1024]{2,1,0:T(8,128)S(1)}, u32[]{:S(2)}, u32[]{:S(2)}) collective-permute-start(f32[8,64,1024]{2,1,0:T(8,128)} %multiply_add_fusion.5), channel_id=1, source_target_pairs={{0,32},{32,64},{64,96},{1,33},{33,65},{65,97},{2,34},{34,66},{66,9... | collective-permute-start | bytes 6291464 | tf_op jit(solution)/shard_map/ppermute | solution.py:31
  210.6 7.6 %collective-permute-start.15 = (f32[8,1,1024]{2,1,0:T(1,128)S(1)}, f32[8,1,1024]{2,1,0:T(1,128)S(1)}, u32[]{:S(2)}, u32[]{:S(2)}) collective-permute-start(f32[8,1,1024]{2,1,0:T(1,128)S(1)} %get-tuple-element.5), channel_id=1, source_target_pairs={{0,2},{2,4},{4,6},{6,8},{8,10},{10,12},{12,14},{14,16},{16,18},{18... | collective-permute-start | bytes 98312 | tf_op jit(solution)/shard_map/ppermute | solution.py:19
  216.0 7.8 %copy-start.2 = (f32[8,64,1024]{2,1,0:T(8,128)S(1)}, f32[8,64,1024]{2,1,0:T(8,128)}, u32[]{:S(2)}) copy-start(f32[8,64,1024]{2,1,0:T(8,128)} %copy-done.1) | copy-start | bytes 6291460
  216.1 7.8 %collective-permute-start.16 = (f32[8,1,1024]{2,1,0:T(1,128)S(1)}, f32[8,1,1024]{2,1,0:T(1,128)S(1)}, u32[]{:S(2)}, u32[]{:S(2)}) collective-permute-start(f32[8,1,1024]{2,1,0:T(1,128)S(1)} %get-tuple-element.4), channel_id=1, source_target_pairs={{2,0},{4,2},{6,4},{8,6},{10,8},{12,10},{14,12},{16,14},{18,16},{20... | collective-permute-start | bytes 98312 | tf_op jit(solution)/shard_map/ppermute | solution.py:21
  226.7 31.1 %copy-start.10 = (f32[1,64,16]{1,2,0:T(8,128)S(1)}, f32[1,64,16]{1,2,0:T(8,128)}, u32[]{:S(2)}) copy-start(f32[1,64,16]{1,2,0:T(8,128)} %param.18) | copy-start | bytes 12292
  226.7 31.1 %copy-start.11 = (f32[1,64]{1,0:T(1,128)S(1)}, f32[1,64]{1,0:T(1,128)}, u32[]{:S(2)}) copy-start(f32[1,64]{1,0:T(1,128)} %param.17) | copy-start | bytes 772
  (7 other events, 47.6 us)
where the time goes:
time: 610 us; the launch traced here: 609 us
  blocking collectives  349 us (57%)
  waiting for transfers between devices  135 us (22%)
  starting transfers between devices  54.3 us (9%)
  local copies, waits for them, and re-layouts  43 us (7%)
  other arithmetic  24.3 us (4%)
    psum x1, blocking collectives, per_device(): gram, cross = lax.psum((gram, cross), ('tm', 'space'))  345 us
    ppermute x3, waiting for transfers between devices, shifted(): lax.ppermute(value, axis, [(source, source + steps) for source in range(f...  114 us
    ppermute x7, starting transfers between devices, with_halo(): lax.ppermute(tail, axis, [(i, (i + 1) % count) for i in range(ends)])  32.1 us
    ppermute x7, waiting for transfers between devices, with_halo(): lax.ppermute(head, axis, [((i + 1) % count, i) for i in range(ends)])  21.2 us
    add x1, local copies, waits for them, and re-layouts, per_device(): running = correction + advance(padded, coeffs, own_rows, coarse_dt, None)  17.9 us
    ppermute x3, starting transfers between devices, shifted(): lax.ppermute(value, axis, [(source, source + steps) for source in range(f...  12.7 us
  transfers between devices with their start and end apart: 17, of which 9 were waited for; matrix products, arithmetic and copies ran while one was open for 2% of the time, Pallas kernels for 0%

commit v1 on v0

--- a/solution.py
+++ b/solution.py
@@ -6,6 +6,12 @@
 
 FINE = 4
 FINE_DT = 0.25
+
+
+def return_all_chunk(view):
+    for c in ("tm", "space"):
+        view = lax.psum(view, c)
+    return view
 
 
 def with_halo(cells, sides, width):
@@ -105,7 +111,7 @@
     misfit = (obs_data[0][None, :] + obs_noise[0].T - every_pred) * inv_spread
     gram = jnp.dot(anomaly, anomaly.T, precision=lax.Precision.HIGHEST)
     cross = jnp.dot(anomaly, misfit.T, precision=lax.Precision.HIGHEST)
-    gram, cross = lax.psum((gram, cross), ("tm", "space"))
+    gram, cross = return_all_chunk((gram, cross))
     system = jnp.eye(total, dtype=jnp.float32) + gram
     factor = jnp.linalg.cholesky(system)
     weights = jax.scipy.linalg.cho_solve((factor, True), cross)

time: 610 us -> 355 us (0.58)
  blocking collectives: 349 us -> 94.6 us
    psum x1 -> x2, blocking collectives: 345 us -> 91 us  [return_all_chunk(): view = lax.psum(view, c)]
  transfers between devices with their start and end apart: 17 -> 17, of which waited for: 9 -> 9; matrix products, arithmetic and copies ran while one was open for 2% -> 4% of each run, Pallas kernels for 0% -> 0%
where the time goes in v1:
time: 355 us; the launch traced here: 354 us
  waiting for transfers between devices  135 us (38%)
  blocking collectives  94.6 us (27%)
  starting transfers between devices  54.3 us (15%)
  local copies, waits for them, and re-layouts  43.1 us (12%)
  other arithmetic  24.3 us (7%)
    ppermute x3, waiting for transfers between devices, shifted(): lax.ppermute(value, axis, [(source, source + steps) for source in range(f...  114 us
    psum x2, blocking collectives, return_all_chunk(): view = lax.psum(view, c)  91 us
    ppermute x7, starting transfers between devices, with_halo(): lax.ppermute(tail, axis, [(i, (i + 1) % count) for i in range(ends)])  32.1 us
    ppermute x7, waiting for transfers between devices, with_halo(): lax.ppermute(head, axis, [((i + 1) % count, i) for i in range(ends)])  21.2 us
    add x1, local copies, waits for them, and re-layouts, per_device(): running = correction + advance(padded, coeffs, own_rows, coarse_dt, None)  18 us
    ppermute x3, starting transfers between devices, shifted(): lax.ppermute(value, axis, [(source, source + steps) for source in range(f...  12.7 us
    gather x1, local copies, waits for them, and re-layouts, per_device(): predicted = jnp.take(flat, local_cell, axis=1)  11.1 us
    slice x7, local copies, waits for them, and re-layouts, advance(): west_cell = jnp.pad(middle[:, :, :-1], ((0, 0), (0, 0), (1, 0)))  10.1 us
  transfers between devices with their start and end apart: 17, of which 9 were waited for; matrix products, arithmetic and copies ran while one was open for 4% of the time, Pallas kernels for 0%

profile of v1, /device:TPU:0, one launch (start us, length us, event | category | flops | bytes accessed | tf_op | source)
XLA Modules:
  0.0 354.4 jit_solution(2229672048806556619)
XLA Ops:
  1.7 3.6 %collective-permute-start = (f32[8,1,1024]{2,1,0:T(1,128)S(1)}, f32[8,1,1024]{2,1,0:T(1,128)S(1)}, u32[]{:S(2)}, u32[]{:S(2)}) collective-permute-start(f32[8,1,1024]{2,1,0:T(1,128)S(1)} %get-tuple-element.33), channel_id=1, source_target_pairs={{0,2},{2,4},{4,6},{6,8},{8,10},{10,12},{12,14},{14,16},{16,18},{18... | collective-permute-start | bytes 98312 | tf_op jit(solution)/shard_map/ppermute | solution.py:25
  6.7 5.1 %fusion.52 = (f32[8,64,1023]{2,1,0:T(8,128)}, f32[8,64,1023]{2,1,0:T(8,128)}) fusion(f32[8,64,1024]{2,1,0:T(8,128)} %bitcast.40), kind=kLoop, calls=%fused_computation.96 | loop fusion | bytes 8380416 | tf_op jit(solution)/shard_map/slice | solution.py:44
  17.7 4.5 %collective-permute-start.2 = (f32[8,1,1024]{2,1,0:T(1,128)S(1)}, f32[8,1,1024]{2,1,0:T(1,128)S(1)}, u32[]{:S(2)}, u32[]{:S(2)}) collective-permute-start(f32[8,1,1024]{2,1,0:T(1,128)S(1)} %get-tuple-element.27), channel_id=1, source_target_pairs={{0,2},{2,4},{4,6},{6,8},{8,10},{10,12},{12,14},{14,16},{16,18},{18... | collective-permute-start | bytes 98312 | tf_op jit(solution)/shard_map/ppermute | solution.py:25
  24.4 3.7 %collective-permute-done.3 = f32[8,1,1024]{2,1,0:T(1,128)S(1)} collective-permute-done((f32[8,1,1024]{2,1,0:T(1,128)S(1)}, f32[8,1,1024]{2,1,0:T(1,128)S(1)}, u32[]{:S(2)}, u32[]{:S(2)}) %collective-permute-start.3) | collective-permute-done | bytes 32800 | tf_op jit(solution)/shard_map/ppermute | solution.py:27
  30.2 3.5 collective-permute-start.4
  35.8 4.6 %collective-permute-done.5 = f32[8,1,1024]{2,1,0:T(1,128)S(1)} collective-permute-done((f32[8,1,1024]{2,1,0:T(1,128)S(1)}, f32[8,1,1024]{2,1,0:T(1,128)S(1)}, u32[]{:S(2)}, u32[]{:S(2)}) %collective-permute-start.5) | collective-permute-done | bytes 32800 | tf_op jit(solution)/shard_map/ppermute | solution.py:27
  42.6 6.0 %collective-permute-start.6 = (f32[8,1,1024]{2,1,0:T(1,128)S(1)}, f32[8,1,1024]{2,1,0:T(1,128)S(1)}, u32[]{:S(2)}, u32[]{:S(2)}) collective-permute-start(f32[8,1,1024]{2,1,0:T(1,128)S(1)} %get-tuple-element.19), channel_id=1, source_target_pairs={{0,2},{2,4},{4,6},{6,8},{8,10},{10,12},{12,14},{14,16},{16,18},{18... | collective-permute-start | bytes 98312 | tf_op jit(solution)/shard_map/ppermute | solution.py:25
  51.0 3.7 %collective-permute-done.7 = f32[8,1,1024]{2,1,0:T(1,128)S(1)} collective-permute-done((f32[8,1,1024]{2,1,0:T(1,128)S(1)}, f32[8,1,1024]{2,1,0:T(1,128)S(1)}, u32[]{:S(2)}, u32[]{:S(2)}) %collective-permute-start.7) | collective-permute-done | bytes 32800 | tf_op jit(solution)/shard_map/ppermute | solution.py:27
  54.7 4.7 %subtract_select_fusion = f32[8,64,1024]{2,1,0:T(8,128)S(1)} fusion(f32[8,64,1024]{2,1,0:T(8,128)S(1)} %fusion.8, f32[8,64,1024]{2,1,0:T(8,128)S(1)} %bitcast.42, f32[8,64,1023]{2,1,0:T(8,128)S(1)} %get-tuple-element.21, f32[8,64,1023]{2,1,0:T(8,128)S(1)} %get-tuple-element.20, f32[8,1,1024]{2,1,0:T(1,128)S(1)} %collective-permute-done.6, ...), kind=kLoop, calls=%fused_computation.5 | loop fusion | flops 21495808 | bytes 15884545 | tf_op jit(solution)/shard_map/jit(_where)/select_n | solution.py:92
  59.4 3.5 collective-permute-start.8
  63.0 40.2 %collective-permute-done.8 = f32[8,64,1024]{2,1,0:T(8,128)S(1)} collective-permute-done((f32[8,64,1024]{2,1,0:T(8,128)S(1)}, f32[8,64,1024]{2,1,0:T(8,128)S(1)}, u32[]{:S(2)}, u32[]{:S(2)}) %collective-permute-start.8) | collective-permute-done | bytes 2097184 | tf_op jit(solution)/shard_map/ppermute | solution.py:37
  104.5 5.2 %collective-permute-start.9 = (f32[8,1,1024]{2,1,0:T(1,128)S(1)}, f32[8,1,1024]{2,1,0:T(1,128)S(1)}, u32[]{:S(2)}, u32[]{:S(2)}) collective-permute-start(f32[8,1,1024]{2,1,0:T(1,128)S(1)} %get-tuple-element.15), channel_id=1, source_target_pairs={{0,2},{2,4},{4,6},{6,8},{8,10},{10,12},{12,14},{14,16},{16,18},{18... | collective-permute-start | bytes 98312 | tf_op jit(solution)/shard_map/ppermute | solution.py:25
  113.2 4.7 %collective-permute-start.11 = (f32[8,64,1024]{2,1,0:T(8,128)S(1)}, f32[8,64,1024]{2,1,0:T(8,128)S(1)}, u32[]{:S(2)}, u32[]{:S(2)}) collective-permute-start(f32[8,64,1024]{2,1,0:T(8,128)S(1)} %multiply_add_fusion.6), channel_id=1, source_target_pairs={{0,32},{32,64},{64,96},{1,33},{33,65},{65,97},{2,34},{34,66},{66,9... | collective-permute-start | bytes 6291464 | tf_op jit(solution)/shard_map/ppermute | solution.py:37
  118.0 38.7 %collective-permute-done.11 = f32[8,64,1024]{2,1,0:T(8,128)S(1)} collective-permute-done((f32[8,64,1024]{2,1,0:T(8,128)S(1)}, f32[8,64,1024]{2,1,0:T(8,128)S(1)}, u32[]{:S(2)}, u32[]{:S(2)}) %collective-permute-start.11) | collective-permute-done | bytes 2097184 | tf_op jit(solution)/shard_map/ppermute | solution.py:37
  156.7 3.9 %collective-permute-start.12 = (f32[8,1,1024]{2,1,0:T(1,128)S(1)}, f32[8,1,1024]{2,1,0:T(1,128)S(1)}, u32[]{:S(2)}, u32[]{:S(2)}) collective-permute-start(f32[8,1,1024]{2,1,0:T(1,128)S(1)} %get-tuple-element.11), channel_id=1, source_target_pairs={{0,2},{2,4},{4,6},{6,8},{8,10},{10,12},{12,14},{14,16},{16,18},{18... | collective-permute-start | bytes 98312 | tf_op jit(solution)/shard_map/ppermute | solution.py:25
  162.8 3.7 %collective-permute-done.13 = f32[8,1,1024]{2,1,0:T(1,128)S(1)} collective-permute-done((f32[8,1,1024]{2,1,0:T(1,128)S(1)}, f32[8,1,1024]{2,1,0:T(1,128)S(1)}, u32[]{:S(2)}, u32[]{:S(2)}) %collective-permute-start.13) | collective-permute-done | bytes 32800 | tf_op jit(solution)/shard_map/ppermute | solution.py:27
  169.5 4.5 %collective-permute-start.14 = (f32[8,64,1024]{2,1,0:T(8,128)}, f32[8,64,1024]{2,1,0:T(8,128)S(1)}, u32[]{:S(2)}, u32[]{:S(2)}) collective-permute-start(f32[8,64,1024]{2,1,0:T(8,128)} %multiply_add_fusion.5), channel_id=1, source_target_pairs={{0,32},{32,64},{64,96},{1,33},{33,65},{65,97},{2,34},{34,66},{66,9... | collective-permute-start | bytes 6291464 | tf_op jit(solution)/shard_map/ppermute | solution.py:37
  175.9 34.7 %collective-permute-done.14 = f32[8,64,1024]{2,1,0:T(8,128)S(1)} collective-permute-done((f32[8,64,1024]{2,1,0:T(8,128)}, f32[8,64,1024]{2,1,0:T(8,128)S(1)}, u32[]{:S(2)}, u32[]{:S(2)}) %collective-permute-start.14) | collective-permute-done | bytes 2097184 | tf_op jit(solution)/shard_map/ppermute | solution.py:37
  210.6 5.4 %collective-permute-start.15 = (f32[8,1,1024]{2,1,0:T(1,128)S(1)}, f32[8,1,1024]{2,1,0:T(1,128)S(1)}, u32[]{:S(2)}, u32[]{:S(2)}) collective-permute-start(f32[8,1,1024]{2,1,0:T(1,128)S(1)} %get-tuple-element.7), channel_id=1, source_target_pairs={{0,2},{2,4},{4,6},{6,8},{8,10},{10,12},{12,14},{14,16},{16,18},{18... | collective-permute-start | bytes 98312 | tf_op jit(solution)/shard_map/ppermute | solution.py:25
  218.2 5.6 %collective-permute-done.16 = f32[8,1,1024]{2,1,0:T(1,128)S(1)} collective-permute-done((f32[8,1,1024]{2,1,0:T(1,128)S(1)}, f32[8,1,1024]{2,1,0:T(1,128)S(1)}, u32[]{:S(2)}, u32[]{:S(2)}) %collective-permute-start.16) | collective-permute-done | bytes 32800 | tf_op jit(solution)/shard_map/ppermute | solution.py:27
  226.7 18.0 %copy.18 = f32[8,64,1024]{0,2,1:T(8,128)} copy(f32[8,64,1024]{2,1,0:T(8,128)} %multiply_add_fusion.4) | data formatting | bytes 4194304 | tf_op jit(solution)/shard_map/add | solution.py:97
  244.7 11.1 %gather_fusion = f32[64,8]{1,0:T(8,128)S(1)} fusion(f32[8,65536]{0,1:T(8,128)} %bitcast.43, s32[1024]{0:T(1024)S(1)} %pad_clamp_fusion), kind=kCustom, calls=%fused_computation | custom fusion | bytes 4352 | tf_op jit(solution)/shard_map/jit(_take)/gather | solution.py:101
  258.1 17.8 %all-reduce.15 = (f32[16,16]{1,0:T(8,128)S(1)}, f32[16,16]{1,0:T(8,128)S(1)}) all-reduce(f32[16,16]{1,0:T(8,128)S(1)} %fusion.21, f32[16,16]{1,0:T(8,128)S(1)} %fusion.29), channel_id=1, replica_groups=mesh['tm'=4,'space'=16,'ens'=2] {'tm'}, use_global_device_ids=true, to_apply=%region_5.6 | all-reduce | flops 512 | bytes 4096 | tf_op jit(solution)/shard_map/psum | solution.py:13
  275.9 73.2 %all-reduce.14 = (f32[16,16]{1,0:T(8,128)S(1)}, f32[16,16]{1,0:T(8,128)S(1)}) all-reduce(f32[16,16]{1,0:T(8,128)S(1)} %get-tuple-element.4, f32[16,16]{1,0:T(8,128)S(1)} %get-tuple-element.5), channel_id=1, replica_groups=mesh['tm'=4,'space'=16,'ens'=2] {'space'}, use_global_device_ids=true, to_apply=%region_6.7 | all-reduce | flops 512 | bytes 4096 | tf_op jit(solution)/shard_map/psum | solution.py:13
  (91 shorter events, 43.6 us)
Async XLA Ops:
  1.7 12.4 %collective-permute-start = (f32[8,1,1024]{2,1,0:T(1,128)S(1)}, f32[8,1,1024]{2,1,0:T(1,128)S(1)}, u32[]{:S(2)}, u32[]{:S(2)}) collective-permute-start(f32[8,1,1024]{2,1,0:T(1,128)S(1)} %get-tuple-element.33), channel_id=1, source_target_pairs={{0,2},{2,4},{4,6},{6,8},{8,10},{10,12},{12,14},{14,16},{16,18},{18... | collective-permute-start | bytes 98312 | tf_op jit(solution)/shard_map/ppermute | solution.py:25
  5.3 8.9 %collective-permute-start.1 = (f32[8,1,1024]{2,1,0:T(1,128)S(1)}, f32[8,1,1024]{2,1,0:T(1,128)S(1)}, u32[]{:S(2)}, u32[]{:S(2)}) collective-permute-start(f32[8,1,1024]{2,1,0:T(1,128)S(1)} %get-tuple-element.32), channel_id=1, source_target_pairs={{2,0},{4,2},{6,4},{8,6},{10,8},{12,10},{14,12},{16,14},{18,16},{20... | collective-permute-start | bytes 98312 | tf_op jit(solution)/shard_map/ppermute | solution.py:27
  6.6 7.6 %copy-start = (f32[1,8,64,1024]{3,2,1,0:T(8,128)S(1)}, f32[1,8,64,1024]{3,2,1,0:T(8,128)}, u32[]{:S(2)}) copy-start(f32[1,8,64,1024]{3,2,1,0:T(8,128)} %param.10) | copy-start | bytes 6291460
  17.7 6.7 %collective-permute-start.2 = (f32[8,1,1024]{2,1,0:T(1,128)S(1)}, f32[8,1,1024]{2,1,0:T(1,128)S(1)}, u32[]{:S(2)}, u32[]{:S(2)}) collective-permute-start(f32[8,1,1024]{2,1,0:T(1,128)S(1)} %get-tuple-element.27), channel_id=1, source_target_pairs={{0,2},{2,4},{4,6},{6,8},{8,10},{10,12},{12,14},{14,16},{16,18},{18... | collective-permute-start | bytes 98312 | tf_op jit(solution)/shard_map/ppermute | solution.py:25
  22.3 5.8 %collective-permute-start.3 = (f32[8,1,1024]{2,1,0:T(1,128)S(1)}, f32[8,1,1024]{2,1,0:T(1,128)S(1)}, u32[]{:S(2)}, u32[]{:S(2)}) collective-permute-start(f32[8,1,1024]{2,1,0:T(1,128)S(1)} %get-tuple-element.26), channel_id=1, source_target_pairs={{2,0},{4,2},{6,4},{8,6},{10,8},{12,10},{14,12},{16,14},{18,16},{20... | collective-permute-start | bytes 98312 | tf_op jit(solution)/shard_map/ppermute | solution.py:27
  30.2 5.6 %collective-permute-start.4 = (f32[8,1,1024]{2,1,0:T(1,128)S(1)}, f32[8,1,1024]{2,1,0:T(1,128)S(1)}, u32[]{:S(2)}, u32[]{:S(2)}) collective-permute-start(f32[8,1,1024]{2,1,0:T(1,128)S(1)} %get-tuple-element.23), channel_id=1, source_target_pairs={{0,2},{2,4},{4,6},{6,8},{8,10},{10,12},{12,14},{14,16},{16,18},{18... | collective-permute-start | bytes 98312 | tf_op jit(solution)/shard_map/ppermute | solution.py:25
  33.7 6.8 %collective-permute-start.5 = (f32[8,1,1024]{2,1,0:T(1,128)S(1)}, f32[8,1,1024]{2,1,0:T(1,128)S(1)}, u32[]{:S(2)}, u32[]{:S(2)}) collective-permute-start(f32[8,1,1024]{2,1,0:T(1,128)S(1)} %get-tuple-element.22), channel_id=1, source_target_pairs={{2,0},{4,2},{6,4},{8,6},{10,8},{12,10},{14,12},{16,14},{18,16},{20... | collective-permute-start | bytes 98312 | tf_op jit(solution)/shard_map/ppermute | solution.py:27
  42.6 8.5 %collective-permute-start.6 = (f32[8,1,1024]{2,1,0:T(1,128)S(1)}, f32[8,1,1024]{2,1,0:T(1,128)S(1)}, u32[]{:S(2)}, u32[]{:S(2)}) collective-permute-start(f32[8,1,1024]{2,1,0:T(1,128)S(1)} %get-tuple-element.19), channel_id=1, source_target_pairs={{0,2},{2,4},{4,6},{6,8},{8,10},{10,12},{12,14},{14,16},{16,18},{18... | collective-permute-start | bytes 98312 | tf_op jit(solution)/shard_map/ppermute | solution.py:25
  48.6 6.1 %collective-permute-start.7 = (f32[8,1,1024]{2,1,0:T(1,128)S(1)}, f32[8,1,1024]{2,1,0:T(1,128)S(1)}, u32[]{:S(2)}, u32[]{:S(2)}) collective-permute-start(f32[8,1,1024]{2,1,0:T(1,128)S(1)} %get-tuple-element.18), channel_id=1, source_target_pairs={{2,0},{4,2},{6,4},{8,6},{10,8},{12,10},{14,12},{16,14},{18,16},{20... | collective-permute-start | bytes 98312 | tf_op jit(solution)/shard_map/ppermute | solution.py:27
  59.4 107.1 %copy-start.1 = (f32[8,64,1024]{2,1,0:T(8,128)}, f32[8,64,1024]{2,1,0:T(8,128)S(1)}, u32[]{:S(2)}) copy-start(f32[8,64,1024]{2,1,0:T(8,128)S(1)} %subtract_select_fusion) | copy-start | bytes 6291460
  59.4 43.7 %collective-permute-start.8 = (f32[8,64,1024]{2,1,0:T(8,128)S(1)}, f32[8,64,1024]{2,1,0:T(8,128)S(1)}, u32[]{:S(2)}, u32[]{:S(2)}) collective-permute-start(f32[8,64,1024]{2,1,0:T(8,128)S(1)} %subtract_select_fusion), channel_id=1, source_target_pairs={{0,32},{32,64},{64,96},{1,33},{33,65},{65,97},{2,34},{34,66},{66,9... | collective-permute-start | bytes 6291464 | tf_op jit(solution)/shard_map/ppermute | solution.py:37
  103.2 7.3 %collective-permute-start.10 = (f32[8,1,1024]{2,1,0:T(1,128)S(1)}, f32[8,1,1024]{2,1,0:T(1,128)S(1)}, u32[]{:S(2)}, u32[]{:S(2)}) collective-permute-start(f32[8,1,1024]{2,1,0:T(1,128)S(1)} %get-tuple-element.14), channel_id=1, source_target_pairs={{2,0},{4,2},{6,4},{8,6},{10,8},{12,10},{14,12},{16,14},{18,16},{20... | collective-permute-start | bytes 98312 | tf_op jit(solution)/shard_map/ppermute | solution.py:27
  104.5 6.8 %collective-permute-start.9 = (f32[8,1,1024]{2,1,0:T(1,128)S(1)}, f32[8,1,1024]{2,1,0:T(1,128)S(1)}, u32[]{:S(2)}, u32[]{:S(2)}) collective-permute-start(f32[8,1,1024]{2,1,0:T(1,128)S(1)} %get-tuple-element.15), channel_id=1, source_target_pairs={{0,2},{2,4},{4,6},{6,8},{8,10},{10,12},{12,14},{14,16},{16,18},{18... | collective-permute-start | bytes 98312 | tf_op jit(solution)/shard_map/ppermute | solution.py:25
  113.2 43.4 %collective-permute-start.11 = (f32[8,64,1024]{2,1,0:T(8,128)S(1)}, f32[8,64,1024]{2,1,0:T(8,128)S(1)}, u32[]{:S(2)}, u32[]{:S(2)}) collective-permute-start(f32[8,64,1024]{2,1,0:T(8,128)S(1)} %multiply_add_fusion.6), channel_id=1, source_target_pairs={{0,32},{32,64},{64,96},{1,33},{33,65},{65,97},{2,34},{34,66},{66,9... | collective-permute-start | bytes 6291464 | tf_op jit(solution)/shard_map/ppermute | solution.py:37
  156.7 6.1 %collective-permute-start.12 = (f32[8,1,1024]{2,1,0:T(1,128)S(1)}, f32[8,1,1024]{2,1,0:T(1,128)S(1)}, u32[]{:S(2)}, u32[]{:S(2)}) collective-permute-start(f32[8,1,1024]{2,1,0:T(1,128)S(1)} %get-tuple-element.11), channel_id=1, source_target_pairs={{0,2},{2,4},{4,6},{6,8},{8,10},{10,12},{12,14},{14,16},{16,18},{18... | collective-permute-start | bytes 98312 | tf_op jit(solution)/shard_map/ppermute | solution.py:25
  160.7 5.8 %collective-permute-start.13 = (f32[8,1,1024]{2,1,0:T(1,128)S(1)}, f32[8,1,1024]{2,1,0:T(1,128)S(1)}, u32[]{:S(2)}, u32[]{:S(2)}) collective-permute-start(f32[8,1,1024]{2,1,0:T(1,128)S(1)} %get-tuple-element.10), channel_id=1, source_target_pairs={{2,0},{4,2},{6,4},{8,6},{10,8},{12,10},{14,12},{16,14},{18,16},{20... | collective-permute-start | bytes 98312 | tf_op jit(solution)/shard_map/ppermute | solution.py:27
  166.5 9.3 %copy-start.12 = (s32[1,64]{1,0:T(1,128)S(1)}, s32[1,64]{1,0:T(1,128)}, u32[]{:S(2)}) copy-start(s32[1,64]{1,0:T(1,128)} %param.16) | copy-start | bytes 772
  166.5 9.4 %copy-start.13 = (f32[1,64]{1,0:T(1,128)S(1)}, f32[1,64]{1,0:T(1,128)}, u32[]{:S(2)}) copy-start(f32[1,64]{1,0:T(1,128)} %param.19) | copy-start | bytes 772
  169.5 41.1 %collective-permute-start.14 = (f32[8,64,1024]{2,1,0:T(8,128)}, f32[8,64,1024]{2,1,0:T(8,128)S(1)}, u32[]{:S(2)}, u32[]{:S(2)}) collective-permute-start(f32[8,64,1024]{2,1,0:T(8,128)} %multiply_add_fusion.5), channel_id=1, source_target_pairs={{0,32},{32,64},{64,96},{1,33},{33,65},{65,97},{2,34},{34,66},{66,9... | collective-permute-start | bytes 6291464 | tf_op jit(solution)/shard_map/ppermute | solution.py:37
  210.6 7.6 %collective-permute-start.15 = (f32[8,1,1024]{2,1,0:T(1,128)S(1)}, f32[8,1,1024]{2,1,0:T(1,128)S(1)}, u32[]{:S(2)}, u32[]{:S(2)}) collective-permute-start(f32[8,1,1024]{2,1,0:T(1,128)S(1)} %get-tuple-element.7), channel_id=1, source_target_pairs={{0,2},{2,4},{4,6},{6,8},{8,10},{10,12},{12,14},{14,16},{16,18},{18... | collective-permute-start | bytes 98312 | tf_op jit(solution)/shard_map/ppermute | solution.py:25
  216.0 7.8 %copy-start.2 = (f32[8,64,1024]{2,1,0:T(8,128)S(1)}, f32[8,64,1024]{2,1,0:T(8,128)}, u32[]{:S(2)}) copy-start(f32[8,64,1024]{2,1,0:T(8,128)} %copy-done.1) | copy-start | bytes 6291460
  216.1 7.8 %collective-permute-start.16 = (f32[8,1,1024]{2,1,0:T(1,128)S(1)}, f32[8,1,1024]{2,1,0:T(1,128)S(1)}, u32[]{:S(2)}, u32[]{:S(2)}) collective-permute-start(f32[8,1,1024]{2,1,0:T(1,128)S(1)} %get-tuple-element.6), channel_id=1, source_target_pairs={{2,0},{4,2},{6,4},{8,6},{10,8},{12,10},{14,12},{16,14},{18,16},{20... | collective-permute-start | bytes 98312 | tf_op jit(solution)/shard_map/ppermute | solution.py:27
  226.7 31.2 %copy-start.10 = (f32[1,64,16]{1,2,0:T(8,128)S(1)}, f32[1,64,16]{1,2,0:T(8,128)}, u32[]{:S(2)}) copy-start(f32[1,64,16]{1,2,0:T(8,128)} %param.18) | copy-start | bytes 12292
  226.7 31.2 %copy-start.11 = (f32[1,64]{1,0:T(1,128)S(1)}, f32[1,64]{1,0:T(1,128)}, u32[]{:S(2)}) copy-start(f32[1,64]{1,0:T(1,128)} %param.17) | copy-start | bytes 772
  (7 other events, 47.6 us)
